TPU v7x, 128 devices: a whole 4x4x4 slice. The times are simulated.
128 devices in a mesh: frow: 16 (over y, z), fcol: 8 (over x, core).
Axes of the slice: x: 4, y: 4, z: 4, core: 2. Of those that a mesh axis runs over, the one named last changes fastest.
Arguments:
- front_orig: float32 [16, 1024, 8, 2048], P('frow', None, 'fcol'), may hold values from -0.1 to 45, as said below
- child_tiles: bfloat16 [8192, 128, 128], P(('frow', 'fcol')), may hold values from -0.25 to 0.25
- tile_target: int32 [8192, 2], P(('frow', 'fcol')), may hold values from 0 to 127, as said below
- tile_rows: int32 [8192, 128], P(('frow', 'fcol')), may hold values from 0 to 127, each once within a row
- tile_cols: int32 [8192, 128], P(('frow', 'fcol')), may hold values from 0 to 127, each once within a row
Outputs:
- front_out: float32 [16, 1024, 8, 2048], P('frow', None, 'fcol')
Inputs may be any that keep to these rules, and one draw needn't show every extreme that they name: `front_orig`: Symmetric; the lower triangle of the front after every tile is added defines a positive definite matrix. `tile_target`: rows come 64 to a device in device order. Column 0 is the owner, frow index times 8 plus fcol index; column 1 the local block on that owner, local block row times 16 plus local block column; the block lies on or below the front's block diagonal. At most 2 tiles of one device go to one owner, and one owner receives exactly 2 from every device.
All inputs are finite; a program needn't handle non-finite values.
Results may differ from a plain program's by a relative error of at most 0.0003.
Values may be sent and summed in bfloat16 or wider, within the bound.
No kernel may reach another device: no remote copies, remote signals or barrier semaphores. Data moves between devices by JAX's collectives and lax.ppermute only.
A program may use at most 128 MiB of HBM per device.

v0:
```python
import jax
import jax.numpy as jnp
from jax import lax
from jax.sharding import PartitionSpec as P

PW = 512
NPANEL = 2
CAP = 2


def as_sent(x):
    return jax.tree.map(lambda a: a.astype(jnp.bfloat16) if a.dtype == jnp.float32 else a, x)


def broadcast(block, axis, source):
    block = jnp.where(lax.axis_index(axis) == source, block, jnp.zeros_like(block))
    return lax.psum(block, axis)


def place_tiles(received):
    tile_block, perm_block, target_block = received
    width = tile_block.shape[-1]
    positions = jnp.arange(width, dtype=jnp.int32)
    row_onehot = (perm_block[:, :, 0, None, :] == positions[:, None]).astype(jnp.bfloat16)
    col_onehot = (perm_block[:, :, 1, None, :] == positions[:, None]).astype(jnp.bfloat16)
    moved = jnp.einsum(
        "abxi,abij->abxj", row_onehot, tile_block, preferred_element_type=jnp.float32
    ).astype(jnp.bfloat16)
    placed = jnp.einsum(
        "abxj,abyj->abxy", moved, col_onehot, preferred_element_type=jnp.float32
    ).astype(jnp.bfloat16)
    return (placed, target_block)


def subtract_product(matrix, row_factor, col_factor):
    product = jnp.dot(
        row_factor, col_factor.T, precision=lax.Precision.HIGH, preferred_element_type=jnp.float32
    )
    return matrix - product


def shards(front_orig, child_tiles, tile_target, tile_rows, tile_cols):
    row_devs = lax.axis_size("frow")
    col_devs = lax.axis_size("fcol")
    owners = row_devs * col_devs
    row_here = lax.axis_index("frow")
    col_here = lax.axis_index("fcol")
    width = child_tiles.shape[1]
    held = child_tiles.shape[0]
    slot_count = owners * CAP
    owner_of = tile_target[:, 0]
    block_of = tile_target[:, 1]
    tile_order = jnp.arange(held, dtype=jnp.int32)
    same_owner = owner_of[:, None] == owner_of[None, :]
    earlier = tile_order[None, :] < tile_order[:, None]
    rank_of = jnp.sum(jnp.where(same_owner & earlier, 1, 0), axis=1).astype(jnp.int32)
    slot_of = owner_of * CAP + rank_of
    slot_match = slot_of[None, :] == jnp.arange(slot_count, dtype=jnp.int32)[:, None]
    source_tile = jnp.sum(jnp.where(slot_match, tile_order[None, :], 0), axis=1)
    filled = jnp.any(slot_match, axis=1)
    own_perms = jnp.stack([tile_rows, tile_cols], axis=1)
    placed_here, _ = place_tiles((child_tiles[None], own_perms[None], block_of[None]))
    placed_here = placed_here[0]
    send_tiles = jnp.where(
        filled[:, None, None],
        jnp.take(placed_here, source_tile, axis=0),
        jnp.zeros((), jnp.bfloat16),
    )
    send_blocks = jnp.where(filled, jnp.take(block_of, source_tile, axis=0), -1)
    placed = lax.all_to_all(
        send_tiles.reshape(owners, CAP, width, width),
        ("frow", "fcol"),
        split_axis=0,
        concat_axis=0,
        tiled=True,
    )
    blocks_in = lax.all_to_all(
        send_blocks.reshape(owners, CAP), ("frow", "fcol"), split_axis=0, concat_axis=0, tiled=True
    )
    local = front_orig[0, :, 0, :]
    row_blocks = local.shape[0] // width
    col_blocks = local.shape[1] // width
    block_ids = jnp.arange(row_blocks * col_blocks, dtype=jnp.int32)
    block_onehot = (blocks_in.reshape(1, slot_count) == block_ids[:, None]).astype(jnp.bfloat16)
    summed = jnp.dot(
        block_onehot, placed.reshape(slot_count, width * width), preferred_element_type=jnp.float32
    )
    added = (
        summed.reshape(row_blocks, col_blocks, width, width)
        .transpose(0, 2, 1, 3)
        .reshape(local.shape)
    )
    matrix = local + added
    first_ids = jnp.arange(row_blocks, dtype=jnp.int32) * col_blocks
    first_onehot = (blocks_in.reshape(1, slot_count) == first_ids[:, None]).astype(jnp.bfloat16)
    first_added = jnp.dot(
        first_onehot, placed.reshape(slot_count, width * width), preferred_element_type=jnp.float32
    ).reshape(local.shape[0], width)
    first_column = local[:, :width] + first_added
    local_rows = jnp.arange(local.shape[0], dtype=jnp.int32)
    local_cols = jnp.arange(local.shape[1], dtype=jnp.int32)
    global_rows = (local_rows // width * row_devs + row_here) * width + local_rows % width
    global_cols = (local_cols // width * col_devs + col_here) * width + local_cols % width
    total = NPANEL * PW
    hi = lax.Precision.HIGH
    first_row = lax.all_gather(
        first_column[:width].astype(jnp.bfloat16), "fcol", axis=1, tiled=True
    )[:, :total]
    split = total // 2
    left = lax.all_gather(first_row[:, :split], "frow", axis=0, tiled=True)[:total]
    left, right_src, matrix = lax.optimization_barrier((left, first_row[:, split:], matrix))
    right = lax.all_gather(right_src, "frow", axis=0, tiled=True)[:total]
    right, own_column = lax.optimization_barrier((right, first_column))
    halves = [left.astype(jnp.float32), right.astype(jnp.float32)]
    row_panel = lax.all_gather(own_column.astype(jnp.bfloat16), "fcol", axis=1, tiled=True)[
        :, :total
    ]
    half = row_devs // col_devs
    pairs = []
    for src_row in range(row_devs):
        for src_col in range(col_devs):
            dst_row = src_row // col_devs * col_devs + src_col
            dst_col = src_row % col_devs
            pairs.append((src_row * col_devs + src_col, dst_row * col_devs + dst_col))
    piece = lax.dynamic_slice_in_dim(row_panel, col_here * width, width, axis=0)
    piece = lax.ppermute(piece, ("frow", "fcol"), pairs)
    col_all = lax.all_gather(piece, "frow", axis=0, tiled=False)
    col_panel = (
        col_all.reshape(half, row_blocks, width, total)
        .transpose(1, 0, 2, 3)
        .reshape(local.shape[1], total)
    )
    rows_all = jnp.concatenate([row_panel, col_panel], axis=0).astype(jnp.float32)
    n_own = local.shape[0]
    full = lax.Precision.HIGHEST
    corner_blocks = total // width
    factor_full = jnp.zeros((total, total), jnp.float32)
    eye = jnp.eye(width, dtype=jnp.float32)
    inverses = []
    for h, cur in enumerate(halves):
        if h > 0:
            done_cols = factor_full[:, : h * split]
            cur = cur - jnp.dot(
                done_cols,
                done_cols[h * split : (h + 1) * split].T,
                precision=full,
                preferred_element_type=jnp.float32,
            )
        for b in range(split // width):
            start = h * split + b * width
            stop = start + width
            lb = b * width
            diag_block = cur[start:stop, lb : lb + width]
            symmetric = jnp.tril(diag_block) + jnp.tril(diag_block, -1).T
            factor = jnp.linalg.cholesky(symmetric)
            inverse = lax.linalg.triangular_solve(factor, eye, left_side=True, lower=True)
            inverses.append(inverse)
            factor_full = factor_full.at[start:stop, start:stop].set(factor)
            if stop < total:
                below = jnp.dot(
                    cur[stop:, lb : lb + width],
                    inverse.T,
                    precision=full,
                    preferred_element_type=jnp.float32,
                )
                factor_full = factor_full.at[stop:, start:stop].set(below)
                if lb + width < split:
                    cur = cur.at[stop:, lb + width :].add(
                        -jnp.dot(
                            below,
                            below[: split - lb - width].T,
                            precision=full,
                            preferred_element_type=jnp.float32,
                        )
                    )
    inv_blocks = jnp.stack(inverses)
    size = width
    while size < total:
        pairs_n = total // (2 * size)
        lower_left = jnp.stack(
            [
                factor_full[
                    (2 * k + 1) * size : (2 * k + 2) * size, 2 * k * size : (2 * k + 1) * size
                ]
                for k in range(pairs_n)
            ]
        )
        upper_inv = inv_blocks[0::2]
        lower_inv = inv_blocks[1::2]
        mixed = -jnp.einsum(
            "nab,nbc->nac",
            lower_inv,
            jnp.einsum("nab,nbc->nac", lower_left, upper_inv, precision=full),
            precision=full,
        )
        zeros = jnp.zeros_like(mixed)
        top = jnp.concatenate([upper_inv, zeros], axis=2)
        bottom = jnp.concatenate([mixed, lower_inv], axis=2)
        inv_blocks = jnp.concatenate([top, bottom], axis=1)
        size *= 2
    factor_inverse = inv_blocks[0]
    solved = jnp.dot(rows_all, factor_inverse.T, precision=hi, preferred_element_type=jnp.float32)
    row_factor = solved[:n_own]
    col_factor = solved[n_own:]
    matrix = subtract_product(matrix, row_factor, col_factor)
    corner_rows = lax.dynamic_slice_in_dim(
        factor_full, jnp.minimum(row_here, total // width - 1) * width, width, axis=0
    )
    head = jnp.where(row_here * width < total, corner_rows, row_factor[:width])
    panel_vals = jnp.concatenate([head, row_factor[width:]], axis=0)
    own_part = lax.dynamic_slice_in_dim(panel_vals, col_here * width, width, axis=1)
    matrix = matrix.at[:, :width].set(own_part)
    lower_part = global_rows[:, None] >= global_cols[None, :]
    result = jnp.where(lower_part, matrix, 0.0)
    return result[None, :, None, :]


def solution(mesh):
    return jax.shard_map(
        shards,
        mesh=mesh,
        in_specs=(
            P("frow", None, "fcol", None),
            P(("frow", "fcol"), None, None),
            P(("frow", "fcol"), None),
            P(("frow", "fcol"), None),
            P(("frow", "fcol"), None),
        ),
        out_specs=P("frow", None, "fcol", None),
        check_vma=False,
    )
```

profile of v0, /device:TPU:23, one launch (start us, length us, event | category | flops | bytes accessed | tf_op | source)
XLA Modules:
  0.0 611.7 jit_solution(1710537951863947196)
XLA Ops:
  11.4 10.6 %all-to-all-start = ((s32[128,1,2]{2,1,0:T(1,128)}), s32[128,1,2]{2,1,0:T(1,128)S(1)}, u32[]{:S(2)}, u32[]{:S(2)}) async-start(s32[128,1,2]{2,1,0:T(1,128)} %bitcast.5), calls=%async_computation | async-start | bytes 131072 | tf_op jit(solution)/shard_map/all_to_all | solution.py:77
  23.1 3.6 fusion.28
  26.8 10.2 %gather_fusion.1 = bf16[256,128,128]{2,1,0:T(8,128)(2,1)} fusion(bf16[64,128,128]{2,1,0:T(8,128)(2,1)} %fusion.28, s32[1024]{0:T(1024)S(1)} %pad_clamp_fusion), kind=kCustom, calls=%fused_computation.1 | custom fusion | bytes 16778240 | tf_op jit(solution)/shard_map/jit(_take)/gather | solution.py:66
  37.0 7.4 %select_select_fusion = bf16[128,2,128,128]{3,2,1,0:T(8,128)(2,1)} fusion(bf16[128,2,128,128]{3,2,1,0:T(8,128)(2,1)} %bitcast.217, pred[128,2]{1,0:T(8,128)(4,1)S(1)} %compare_and_fusion, pred[128,2]{1,0:T(8,128)(4,1)S(1)} %broadcast_in_dim.106), kind=kLoop, calls=%fused_computation.7 | loop fusion | flops 8388608 | bytes 16777728 | tf_op jit(solution)/shard_map/jit(_where)/select_n | solution.py:64
  44.4 10.2 %all-to-all-start.1 = ((bf16[128,2,128,128]{3,2,1,0:T(8,128)(2,1)}), bf16[128,2,128,128]{3,2,1,0:T(8,128)(2,1)}, u32[]{:S(2)}, u32[]{:S(2)}) async-start(bf16[128,2,128,128]{3,2,1,0:T(8,128)(2,1)} %select_select_fusion), calls=%async_computation.1 | async-start | bytes 16777216 | tf_op jit(solution)/shard_map/all_to_all | solution.py:70
  55.0 20.7 %copy.246 = f32[1,1024,1,2048]{1,3,2,0:T(8,128)} copy(f32[1,1024,1,2048]{3,2,1,0:T(1,128)} %param.52) | data formatting | bytes 16777216 | tf_op args[0]
  77.0 76.1 %all-to-all-done.1 = bf16[128,2,128,128]{3,2,1,0:T(8,128)(2,1)} async-done(((bf16[128,2,128,128]{3,2,1,0:T(8,128)(2,1)}), bf16[128,2,128,128]{3,2,1,0:T(8,128)(2,1)}, u32[]{:S(2)}, u32[]{:S(2)}) %all-to-all-start.1) | async-done | bytes 8388640 | tf_op jit(solution)/shard_map/all_to_all | solution.py:70
  153.1 7.8 %fusion.143 = f32[8,16384]{1,0:T(8,128)S(1)} fusion(s32[256]{0:T(256)S(1)} %eq.128, s32[8]{0:T(128)S(1)} %iota_multiply_fusion, bf16[32,8,128,128]{3,2,1,0:T(8,128)(2,1)} %bitcast.76), kind=kOutput, calls=%fused_computation.238 | convolution fusion | flops 67110912 | bytes 8913952 | tf_op jit(solution)/shard_map/dot_general | solution.py:96
  162.4 18.7 %all_gather.18 = bf16[128,1024]{0,1:T(8,128)(2,1)S(1)} all-gather(bf16[128,128]{0,1:T(8,128)(2,1)S(1)} %slice.839), channel_id=1, replica_groups=mesh['frow'=16,'fcol'=8] {'fcol'}, dimensions={1}, use_global_device_ids=true | all-gather | bytes 294912 | tf_op jit(solution)/shard_map/all_gather | solution.py:106
  184.6 23.3 %copy.365 = bf16[32,8,128,128]{3,1,2,0:T(8,128)(2,1)} copy(bf16[32,8,128,128]{3,2,1,0:T(8,128)(2,1)} %bitcast.76) | data formatting | bytes 16777216
  207.9 11.9 %copy.249 = bf16[256,16384]{0,1:T(8,128)(2,1)} copy(bf16[256,16384]{1,0:T(8,128)(2,1)} %bitcast.218) | data formatting | bytes 16777216 | tf_op jit(solution)/shard_map/reshape | solution.py:97
  219.8 6.3 %fusion.90 = f32[8,16,128,128]{3,1,2,0:T(8,128)S(1)} fusion(bf16[128,128,256,1]{2,1,0,3:T(8,128)(2,1)} %bitcast.221, s32[8,16]{1,0:T(8,128)S(1)} %multiply_add_fusion, s32[256]{0:T(256)S(1)} %eq.128), kind=kOutput, calls=%fused_computation.113 | convolution fusion | flops 1073774592 | bytes 16778752 | tf_op jit(solution)/shard_map/dot_general | solution.py:85
  226.1 7.5 %copy.364 = f32[128,8,16,128]{3,1,2,0:T(8,128)} copy(f32[128,8,16,128]{3,2,1,0:T(8,128)S(1)} %bitcast.222) | data formatting | bytes 16777216
  233.6 9.3 %copy.343 = f32[1024,2048]{0,1:T(8,128)} copy(f32[1024,2048]{1,0:T(8,128)} %bitcast.219) | data formatting | bytes 16777216 | tf_op jit(solution)/shard_map/reshape | solution.py:91
  242.9 12.1 %bitcast_add_fusion.16 = f32[1024,2048]{0,1:T(8,128)} fusion(f32[1024,2048]{0,1:T(8,128)} %copy.343, f32[1,1024,1,2048]{1,3,2,0:T(8,128)} %copy.246), kind=kLoop, calls=%fused_computation.280 | loop fusion | flops 2097152 | bytes 25165824 | tf_op jit(solution)/shard_map/add | solution.py:93
  257.4 11.7 %cholesky.134 = f32[128,128]{1,0:T(8,128)S(1)} custom-call(f32[128,128]{1,0:T(8,128)S(1)} %copy.258), custom_call_target="Cholesky" | custom-call | tf_op jit(solution)/shard_map/jit(cholesky)/cholesky | solution.py:155
  270.9 9.8 %custom-call.12 = f32[1,128,128]{1,2,0:T(8,128)S(1)} custom-call(f32[1,128,128]{2,1,0:T(8,128)S(1)} %copy.261), custom_call_target="InvertDiagBlocksLowerTriangular" | custom-call | tf_op jit(solution)/shard_map/triangular_solve/custom-call.0 | solution.py:156
  282.8 2.0 copy.289
  284.8 2.3 fusion.34
  288.2 11.9 %cholesky.145 = f32[128,128]{1,0:T(8,128)S(1)} custom-call(f32[128,128]{1,0:T(8,128)S(1)} %copy.268), custom_call_target="Cholesky" | custom-call | tf_op jit(solution)/shard_map/jit(cholesky)/cholesky | solution.py:155
  300.2 2.5 scatter.54
  305.8 9.8 %custom-call.13 = f32[1,128,128]{1,2,0:T(8,128)S(1)} custom-call(f32[1,128,128]{2,1,0:T(8,128)S(1)} %copy.271), custom_call_target="InvertDiagBlocksLowerTriangular" | custom-call | tf_op jit(solution)/shard_map/triangular_solve/custom-call.0 | solution.py:156
  318.6 11.7 %cholesky.156 = f32[128,128]{1,0:T(8,128)S(1)} custom-call(f32[128,128]{1,0:T(8,128)S(1)} %copy.278), custom_call_target="Cholesky" | custom-call | tf_op jit(solution)/shard_map/jit(cholesky)/cholesky | solution.py:155
  333.5 9.8 %custom-call.14 = f32[1,128,128]{1,2,0:T(8,128)S(1)} custom-call(f32[1,128,128]{2,1,0:T(8,128)S(1)} %copy.281), custom_call_target="InvertDiagBlocksLowerTriangular" | custom-call | tf_op jit(solution)/shard_map/triangular_solve/custom-call.0 | solution.py:156
  346.2 11.7 %cholesky.167 = f32[128,128]{1,0:T(8,128)S(1)} custom-call(f32[128,128]{1,0:T(8,128)S(1)} %fusion.105), custom_call_target="Cholesky" | custom-call | tf_op jit(solution)/shard_map/jit(cholesky)/cholesky | solution.py:155
  361.0 9.8 %custom-call.15 = f32[1,128,128]{1,2,0:T(8,128)S(1)} custom-call(f32[1,128,128]{2,1,0:T(8,128)S(1)} %copy.288), custom_call_target="InvertDiagBlocksLowerTriangular" | custom-call | tf_op jit(solution)/shard_map/triangular_solve/custom-call.0 | solution.py:156
  373.7 5.4 fusion.31
  381.7 11.7 %cholesky.178 = f32[128,128]{1,0:T(8,128)S(1)} custom-call(f32[128,128]{1,0:T(8,128)S(1)} %fusion.103), custom_call_target="Cholesky" | custom-call | tf_op jit(solution)/shard_map/jit(cholesky)/cholesky | solution.py:155
  395.6 9.8 %custom-call.16 = f32[1,128,128]{1,2,0:T(8,128)S(1)} custom-call(f32[1,128,128]{2,1,0:T(8,128)S(1)} %copy.299), custom_call_target="InvertDiagBlocksLowerTriangular" | custom-call | tf_op jit(solution)/shard_map/triangular_solve/custom-call.0 | solution.py:156
  408.1 2.1 collective-permute-start
  412.1 16.0 %collective-permute-done = bf16[128,1024]{0,1:T(8,128)(2,1)S(1)} collective-permute-done((bf16[128,1024]{0,1:T(8,128)(2,1)S(1)}, bf16[128,1024]{0,1:T(8,128)(2,1)S(1)}, u32[]{:S(2)}, u32[]{:S(2)}) %collective-permute-start) | collective-permute-done | bytes 262176 | tf_op jit(solution)/shard_map/ppermute | solution.py:126
  429.0 11.7 %cholesky.189 = f32[128,128]{1,0:T(8,128)S(1)} custom-call(f32[128,128]{1,0:T(8,128)S(1)} %fusion.101), custom_call_target="Cholesky" | custom-call | tf_op jit(solution)/shard_map/jit(cholesky)/cholesky | solution.py:155
  443.7 9.8 %custom-call.17 = f32[1,128,128]{1,2,0:T(8,128)S(1)} custom-call(f32[1,128,128]{2,1,0:T(8,128)S(1)} %copy.305), custom_call_target="InvertDiagBlocksLowerTriangular" | custom-call | tf_op jit(solution)/shard_map/triangular_solve/custom-call.0 | solution.py:156
  454.9 11.7 %cholesky.200 = f32[128,128]{1,0:T(8,128)S(1)} custom-call(f32[128,128]{1,0:T(8,128)S(1)} %fusion.99), custom_call_target="Cholesky" | custom-call | tf_op jit(solution)/shard_map/jit(cholesky)/cholesky | solution.py:155
  469.5 10.0 %custom-call.18 = f32[1,128,128]{1,2,0:T(8,128)S(1)} custom-call(f32[1,128,128]{2,1,0:T(8,128)S(1)} %copy.311), custom_call_target="InvertDiagBlocksLowerTriangular" | custom-call | tf_op jit(solution)/shard_map/triangular_solve/custom-call.0 | solution.py:156
  480.8 11.7 %cholesky.211 = f32[128,128]{1,0:T(8,128)S(1)} custom-call(f32[128,128]{1,0:T(8,128)S(1)} %fusion.97), custom_call_target="Cholesky" | custom-call | tf_op jit(solution)/shard_map/jit(cholesky)/cholesky | solution.py:155
  493.8 9.8 %custom-call.19 = f32[1,128,128]{1,2,0:T(8,128)S(1)} custom-call(f32[1,128,128]{2,1,0:T(8,128)S(1)} %get-tuple-element.281), custom_call_target="InvertDiagBlocksLowerTriangular" | custom-call | tf_op jit(solution)/shard_map/triangular_solve/custom-call.0 | solution.py:156
  510.9 3.5 fusion.42
  517.8 2.9 copy.252
  520.7 5.6 copy.360
  526.2 6.7 %copy.251 = bf16[2,8,128,1024]{3,2,0,1:T(8,128)(2,1)} copy(bf16[2,8,128,1024]{2,1,0,3:T(8,128)(2,1)} %bitcast.220) | data formatting | bytes 8388608 | tf_op jit(solution)/shard_map/reshape | solution.py:129
  532.9 16.6 %fusion.2 = f32[3072,1024]{1,0:T(8,128)S(1)} fusion(bf16[2048,1024]{1,0:T(8,128)(2,1)} %bitcast.224, bf16[1024,1024]{1,0:T(8,128)(2,1)S(1)} %copy.252, f32[1,512,512]{2,1,0:T(8,128)} %get-tuple-element.292, f32[1,512,512]{2,1,0:T(8,128)} %get-tuple-element.291, f32[1,512,512]{2,1,0:T(8,128)S(1)} %fusion.35), kind=kOutput, calls=%fused_computation.8 | convolution fusion | flops 19344130048 | bytes 22020096 | tf_op jit(solution)/shard_map/dot_general | solution.py:202
  549.6 2.3 slice.757
  551.9 17.7 %fusion.15 = f32[1024,2048]{0,1:T(8,128)} fusion(f32[1024,2048]{0,1:T(8,128)} %bitcast_add_fusion.16, f32[3072,1024]{1,0:T(8,128)S(1)} %fusion.2), kind=kOutput, calls=%fused_computation.26 | convolution fusion | flops 12886999040 | bytes 29360128 | tf_op jit(solution)/shard_map/dot_general | solution.py:36
  569.8 5.0 copy.345
  575.9 2.6 fusion.49
  578.5 5.9 select_bitcast_fusion
  584.5 20.5 %copy.329 = f32[1,1024,1,2048]{3,2,1,0:T(1,128)} copy(f32[1,1024,1,2048]{1,3,2,0:T(8,128)} %select_bitcast_fusion) | data formatting | bytes 16777216 | tf_op jit(solution)/shard_map/broadcast_in_dim | solution.py:215
  (208 shorter events, 69.3 us)
Async XLA Ops:
  6.5 16.6 %copy-start = (bf16[64,128,128]{2,1,0:T(8,128)(2,1)S(1)}, bf16[64,128,128]{2,1,0:T(8,128)(2,1)}, u32[]{:S(2)}) copy-start(bf16[64,128,128]{2,1,0:T(8,128)(2,1)} %param.53) | copy-start | bytes 6291460
  11.4 33.0 %all-to-all-start = ((s32[128,1,2]{2,1,0:T(1,128)}), s32[128,1,2]{2,1,0:T(1,128)S(1)}, u32[]{:S(2)}, u32[]{:S(2)}) async-start(s32[128,1,2]{2,1,0:T(1,128)} %bitcast.5), calls=%async_computation | async-start | bytes 131072 | tf_op jit(solution)/shard_map/all_to_all | solution.py:77
  44.4 108.7 %all-to-all-start.1 = ((bf16[128,2,128,128]{3,2,1,0:T(8,128)(2,1)}), bf16[128,2,128,128]{3,2,1,0:T(8,128)(2,1)}, u32[]{:S(2)}, u32[]{:S(2)}) async-start(bf16[128,2,128,128]{3,2,1,0:T(8,128)(2,1)} %select_select_fusion), calls=%async_computation.1 | async-start | bytes 16777216 | tf_op jit(solution)/shard_map/all_to_all | solution.py:70
  54.6 200.4 %all-gather.6.cloned.1.call-start = ((), (), s32[]{:S(2)}) async-start(), calls=%async_computation.2 | async-start | bytes 2228224 | tf_op jit(solution)/shard_map/all_gather | solution.py:110
  162.3 45.6 %copy-start.5 = (bf16[1024,128]{0,1:T(8,128)(2,1)}, bf16[1024,128]{0,1:T(8,128)(2,1)S(1)}, u32[]{:S(2)}) copy-start(bf16[1024,128]{0,1:T(8,128)(2,1)S(1)} %slice_add_fusion) | copy-start | bytes 786436
  181.8 162.5 %all-gather.8.cloned.1.call-start = ((), (), s32[]{:S(2)}) async-start(), calls=%async_computation.3 | async-start | bytes 2228224 | tf_op jit(solution)/shard_map/all_gather | solution.py:112
  181.9 26.0 %copy-start.10 = (s32[128]{0:T(128)}, s32[128]{0:T(128)S(1)}, u32[]{:S(2)}) copy-start(s32[128]{0:T(128)S(1)} %iota_add_fusion) | copy-start | bytes 1540
  182.1 75.1 %copy-start.6 = (pred[128,128]{0,1:T(8,128)(4,1)}, pred[128,128]{0,1:T(8,128)(4,1)S(1)}, u32[]{:S(2)}) copy-start(pred[128,128]{0,1:T(8,128)(4,1)S(1)} %copy.255) | copy-start | bytes 49156
  256.6 150.5 %all-gather.10.cloned.1.call-start = ((), (), s32[]{:S(2)}) async-start(), calls=%async_computation.4 | async-start | bytes 2359296 | tf_op jit(solution)/shard_map/all_gather | solution.py:115
  287.1 16.4 %copy-start.4 = (f32[896,128]{0,1:T(8,128)S(1)}, f32[896,128]{0,1:T(8,128)}, u32[]{:S(2)}) copy-start(f32[896,128]{0,1:T(8,128)} %copy.289) | copy-start | bytes 1376260
  300.2 18.2 %copy-start.7 = (pred[128,128]{0,1:T(8,128)(4,1)S(1)}, pred[128,128]{0,1:T(8,128)(4,1)}, u32[]{:S(2)}) copy-start(pred[128,128]{0,1:T(8,128)(4,1)} %copy-done.6) | copy-start | bytes 49156
  318.3 27.7 %copy-start.11 = (s32[128]{0:T(128)S(1)}, s32[128]{0:T(128)}, u32[]{:S(2)}) copy-start(s32[128]{0:T(128)} %copy-done.10) | copy-start | bytes 1540
  344.3 28.5 %slice-start = ((bf16[2048,512]{0,1:T(8,128)(2,1)}), bf16[1024,512]{0,1:T(8,128)(2,1)S(1)}, s32[]{:S(2)}) async-start(bf16[2048,512]{0,1:T(8,128)(2,1)} %all-gather.8.cloned.1.call-done), calls=%async_computation.6 | async-start | bytes 2097152 | tf_op jit(solution)/shard_map/slice | solution.py:112
  344.3 176.3 %all-gather.12.cloned.1.call-start = ((), (), s32[]{:S(2)}) async-start(), calls=%async_computation.5 | async-start | bytes 4456448 | tf_op jit(solution)/shard_map/all_gather | solution.py:127
  373.7 31.7 %copy-start.3 = (f32[8,128,128]{2,1,0:T(8,128)S(1)}, f32[8,128,128]{2,1,0:T(8,128)}, u32[]{:S(2)}) copy-start(f32[8,128,128]{2,1,0:T(8,128)} %get-tuple-element.321) | copy-start | bytes 1572868
  379.2 1.4 copy-start.2
  408.1 19.9 %collective-permute-start = (bf16[128,1024]{0,1:T(8,128)(2,1)S(1)}, bf16[128,1024]{0,1:T(8,128)(2,1)S(1)}, u32[]{:S(2)}, u32[]{:S(2)}) collective-permute-start(bf16[128,1024]{0,1:T(8,128)(2,1)S(1)} %constant_dynamic-slice_fusion), channel_id=1, source_target_pairs={{0,0},{1,8},{2,16},{3,24},{4,32},{5,40},{6,48},{7,56},{8,1},{9,9},... | collective-permute-start | bytes 786440 | tf_op jit(solution)/shard_map/ppermute | solution.py:126
  428.0 0.7 copy-start.8
  574.8 3.7 copy-start.9
  574.8 3.7 copy-start.12
  578.5 26.4 %copy-start.1 = (bf16[64,128,128]{2,1,0:T(8,128)(2,1)S(1)}, bf16[64,128,128]{2,1,0:T(8,128)(2,1)}, u32[]{:S(2)}) copy-start(bf16[64,128,128]{2,1,0:T(8,128)(2,1)} %param.53) | copy-start | bytes 6291460
Sparse Core Ops, SparseCore 0:
  181.9 45.7 all-gather.5
  256.8 45.8 all-gather.7
  344.4 24.9 all-gather.9
  428.9 53.5 all-gather.11
where the time goes:
time: 620 us; the launch traced here: 612 us
  other arithmetic  227 us (37%)
  local copies, waits for them, and re-layouts  154 us (25%)
  waiting for transfers between devices  92.2 us (15%)
  matrix products  82.1 us (13%)
  starting transfers between devices  24 us (4%)
  blocking collectives  18.7 us (3%)
  between operations  14.5 us (2%)
    another operation x24, other arithmetic, shards(): factor = jnp.linalg.cholesky(symmetric)  100 us
    another operation x11, other arithmetic, shards(): lax.linalg.triangular_solve(factor, eye, left_side=True, lower=True)  80 us
    all_to_all x1, waiting for transfers between devices, shards(): lax.all_to_all(send_tiles.reshape(owners, CAP, width, width), ('frow', 'f...  76.1 us
    unnamed x32, local copies, waits for them, and re-layouts  64.4 us
    broadcast_in_dim x1, local copies, waits for them, and re-layouts, shards(): return result[None, :, None, :]  20.5 us
    all_gather x1, blocking collectives, shards(): lax.all_gather(first_column[:width].astype(jnp.bfloat16), 'fcol', axis=1,...  18.7 us
    dot_general x1, matrix products, subtract_product(): jnp.dot(row_factor, col_factor.T, precision=lax.Precision.HIGH, preferred...  17.7 us
    dot_general x1, matrix products, shards(): jnp.dot(rows_all, factor_inverse.T, precision=hi, preferred_element_type=...  16.6 us
  transfers between devices with their start and end apart: 7, of which 2 were waited for; matrix products, arithmetic and copies ran while one was open for 59% of the time, Pallas kernels for 0%

commit v1 on v0

--- a/solution.py
+++ b/solution.py
@@ -6,6 +6,12 @@
 PW = 512
 NPANEL = 2
 CAP = 2
+
+
+def treat_heads(target, axis_id):
+    return jnp.concatenate(
+        jax.lax.all_to_all(jnp.stack(jax.lax.axis_size(axis_id) * [target]), axis_id, 0, 0), axis=1
+    )
 
 
 def as_sent(x):
@@ -103,9 +109,7 @@
     global_cols = (local_cols // width * col_devs + col_here) * width + local_cols % width
     total = NPANEL * PW
     hi = lax.Precision.HIGH
-    first_row = lax.all_gather(
-        first_column[:width].astype(jnp.bfloat16), "fcol", axis=1, tiled=True
-    )[:, :total]
+    first_row = treat_heads(first_column[:width].astype(jnp.bfloat16), axis_id="fcol")[:, :total]
     split = total // 2
     left = lax.all_gather(first_row[:, :split], "frow", axis=0, tiled=True)[:total]
     left, right_src, matrix = lax.optimization_barrier((left, first_row[:, split:], matrix))

time: 620 us -> 557 us (0.90)
  local copies, waits for them, and re-layouts: 154 us -> 95.4 us
    unnamed x32 -> x22, local copies, waits for them, and re-layouts: 64.4 us -> 41.5 us
    all_gather x1 -> x0, blocking collectives: 18.7 us -> none  [shards(): lax.all_gather(first_column[:width].astype(jnp.bfloat16), 'fcol', axis=1,...]
    all_to_all x0 -> x1, blocking collectives: none -> 14.8 us  [treat_heads(): jax.lax.all_to_all(jnp.stack(jax.lax.axis_size(axis_id) * [target]), axis...]
    ppermute x1, waiting for transfers between devices: 16 us -> 3.89 us  [shards(): piece = lax.ppermute(piece, ('frow', 'fcol'), pairs)]
    all_to_all x1, waiting for transfers between devices: 76.1 us -> 85.8 us  [shards(): lax.all_to_all(send_tiles.reshape(owners, CAP, width, width), ('frow', 'f...]
    reshape x1 -> x0, local copies, waits for them, and re-layouts: 9.27 us -> none  [shards(): added = summed.reshape(row_blocks, col_blocks, width, width).transpose(0,...]
    broadcast_in_dim x1, local copies, waits for them, and re-layouts: 20.5 us -> 12.5 us  [shards(): return result[None, :, None, :]]
    another operation x11 -> x9, other arithmetic: 80 us -> 79.3 us  [shards(): lax.linalg.triangular_solve(factor, eye, left_side=True, lower=True)]
  transfers between devices with their start and end apart: 7 -> 7, of which waited for: 2 -> 2; matrix products, arithmetic and copies ran while one was open for 59% -> 60% of each run, Pallas kernels for 0% -> 0%
where the time goes in v1:
time: 557 us; the launch traced here: 549 us
  other arithmetic  223 us (40%)
  local copies, waits for them, and re-layouts  95.4 us (17%)
  waiting for transfers between devices  89.8 us (16%)
  matrix products  85.8 us (15%)
  starting transfers between devices  26.3 us (5%)
  blocking collectives  14.8 us (3%)
  between operations  14.3 us (3%)
    another operation x24, other arithmetic, shards(): factor = jnp.linalg.cholesky(symmetric)  99.9 us
    all_to_all x1, waiting for transfers between devices, shards(): lax.all_to_all(send_tiles.reshape(owners, CAP, width, width), ('frow', 'f...  85.8 us
    another operation x9, other arithmetic, shards(): lax.linalg.triangular_solve(factor, eye, left_side=True, lower=True)  79.3 us
    unnamed x22, local copies, waits for them, and re-layouts  41.5 us
    dot_general x1, matrix products, subtract_product(): jnp.dot(row_factor, col_factor.T, precision=lax.Precision.HIGH, preferred...  18 us
    add x1, other arithmetic, shards(): matrix = local + added  17.4 us
    all_to_all x1, blocking collectives, treat_heads(): jax.lax.all_to_all(jnp.stack(jax.lax.axis_size(axis_id) * [target]), axis...  14.8 us
    dot_general x1, matrix products, shards(): jnp.dot(rows_all, factor_inverse.T, precision=hi, preferred_element_type=...  14.6 us
  transfers between devices with their start and end apart: 7, of which 2 were waited for; matrix products, arithmetic and copies ran while one was open for 60% of the time, Pallas kernels for 0%

profile of v1, /device:TPU:23, one launch (start us, length us, event | category | flops | bytes accessed | tf_op | source)
XLA Modules:
  0.0 549.3 jit_solution(12780367596143964777)
XLA Ops:
  8.8 1.9 gather_fusion
  11.4 10.6 %all-to-all-start = ((s32[128,1,2]{2,1,0:T(1,128)}), s32[128,1,2]{2,1,0:T(1,128)S(1)}, u32[]{:S(2)}, u32[]{:S(2)}) async-start(s32[128,1,2]{2,1,0:T(1,128)} %bitcast.4), calls=%async_computation | async-start | bytes 131072 | tf_op jit(solution)/shard_map/all_to_all | solution.py:83
  23.1 3.6 fusion.28
  26.8 10.2 %gather_fusion.1 = bf16[256,128,128]{2,1,0:T(8,128)(2,1)} fusion(bf16[64,128,128]{2,1,0:T(8,128)(2,1)} %fusion.28, s32[1024]{0:T(1024)S(1)} %pad_clamp_fusion), kind=kCustom, calls=%fused_computation.1 | custom fusion | bytes 16778240 | tf_op jit(solution)/shard_map/jit(_take)/gather | solution.py:72
  37.0 7.4 %select_select_fusion = bf16[128,2,128,128]{3,2,1,0:T(8,128)(2,1)} fusion(bf16[128,2,128,128]{3,2,1,0:T(8,128)(2,1)} %bitcast.217, pred[128,2]{1,0:T(8,128)(4,1)S(1)} %compare_and_fusion, pred[128,2]{1,0:T(8,128)(4,1)S(1)} %broadcast_in_dim.106), kind=kLoop, calls=%fused_computation.8 | loop fusion | flops 8388608 | bytes 16777728 | tf_op jit(solution)/shard_map/jit(_where)/select_n | solution.py:70
  44.4 10.2 %all-to-all-start.1 = ((bf16[128,2,128,128]{3,2,1,0:T(8,128)(2,1)}), bf16[128,2,128,128]{3,2,1,0:T(8,128)(2,1)}, u32[]{:S(2)}, u32[]{:S(2)}) async-start(bf16[128,2,128,128]{3,2,1,0:T(8,128)(2,1)} %select_select_fusion), calls=%async_computation.1 | async-start | bytes 16777216 | tf_op jit(solution)/shard_map/all_to_all | solution.py:76
  55.2 10.7 %copy.218 = f32[1,1024,1,2048]{3,1,2,0:T(8,128)} copy(f32[1,1024,1,2048]{3,2,1,0:T(1,128)} %param.52) | data formatting | bytes 16777216
  67.3 85.8 %all-to-all-done.1 = bf16[128,2,128,128]{3,2,1,0:T(8,128)(2,1)} async-done(((bf16[128,2,128,128]{3,2,1,0:T(8,128)(2,1)}), bf16[128,2,128,128]{3,2,1,0:T(8,128)(2,1)}, u32[]{:S(2)}, u32[]{:S(2)}) %all-to-all-start.1) | async-done | bytes 8388640 | tf_op jit(solution)/shard_map/all_to_all | solution.py:76
  153.1 7.8 %fusion.139 = f32[8,16384]{1,0:T(8,128)S(1)} fusion(s32[256]{0:T(256)S(1)} %eq.128, s32[8]{0:T(128)S(1)} %iota_multiply_fusion, bf16[32,8,128,128]{3,2,1,0:T(8,128)(2,1)} %bitcast.80), kind=kOutput, calls=%fused_computation.235 | convolution fusion | flops 67110912 | bytes 8913952 | tf_op jit(solution)/shard_map/dot_general | solution.py:102
  162.3 14.8 %all_to_all.16 = bf16[8,128,128]{1,2,0:T(8,128)(2,1)S(1)} all-to-all(bf16[8,128,128]{1,2,0:T(8,128)(2,1)S(1)} %stack.75), channel_id=1, replica_groups=mesh['frow'=16,'fcol'=8] {'fcol'}, dimensions={0} | all-to-all | bytes 524288 | tf_op jit(solution)/shard_map/all_to_all | solution.py:13
  178.3 23.5 %copy.217 = bf16[32,8,128,128]{3,1,2,0:T(8,128)(2,1)} copy(bf16[32,8,128,128]{3,2,1,0:T(8,128)(2,1)} %bitcast.80) | data formatting | bytes 16777216
  201.8 11.9 %copy.142 = bf16[256,16384]{0,1:T(8,128)(2,1)} copy(bf16[256,16384]{1,0:T(8,128)(2,1)} %bitcast.218) | data formatting | bytes 16777216 | tf_op jit(solution)/shard_map/reshape | solution.py:103
  213.8 9.6 %fusion.90 = f32[8,16,128,128]{3,1,2,0:T(8,128)} fusion(bf16[128,128,256,1]{2,1,0,3:T(8,128)(2,1)} %bitcast.221, s32[8,16]{1,0:T(8,128)S(1)} %multiply_add_fusion, s32[256]{0:T(256)S(1)} %eq.128), kind=kOutput, calls=%fused_computation.114 | convolution fusion | flops 1073774592 | bytes 16778752 | tf_op jit(solution)/shard_map/dot_general | solution.py:91
  223.4 17.4 %bitcast_add_fusion = f32[1024,2048]{1,0:T(8,128)} fusion(f32[128,8,16,128]{3,2,1,0:T(8,128)} %bitcast.220, f32[1,1024,1,2048]{3,2,1,0:T(1,128)} %param.52), kind=kLoop, calls=%fused_computation.2 | loop fusion | flops 2097152 | bytes 25165824 | tf_op jit(solution)/shard_map/add | solution.py:99
  240.8 1.3 slice.718
  243.7 11.7 %cholesky.134 = f32[128,128]{1,0:T(8,128)S(1)} custom-call(f32[128,128]{1,0:T(8,128)S(1)} %copy.149), custom_call_target="Cholesky" | custom-call | tf_op jit(solution)/shard_map/jit(cholesky)/cholesky | solution.py:159
  256.8 9.8 %custom-call.12 = f32[1,128,128]{1,2,0:T(8,128)S(1)} custom-call(f32[1,128,128]{2,1,0:T(8,128)S(1)} %get-tuple-element.281), custom_call_target="InvertDiagBlocksLowerTriangular" | custom-call | tf_op jit(solution)/shard_map/triangular_solve/custom-call.0 | solution.py:160
  266.6 2.5 scatter.54
  272.8 12.1 %cholesky.145 = f32[128,128]{1,0:T(8,128)S(1)} custom-call(f32[128,128]{1,0:T(8,128)S(1)} %copy.156), custom_call_target="Cholesky" | custom-call | tf_op jit(solution)/shard_map/jit(cholesky)/cholesky | solution.py:159
  286.8 9.8 %custom-call.13 = f32[1,128,128]{1,2,0:T(8,128)S(1)} custom-call(f32[1,128,128]{2,1,0:T(8,128)S(1)} %get-tuple-element.310), custom_call_target="InvertDiagBlocksLowerTriangular" | custom-call | tf_op jit(solution)/shard_map/triangular_solve/custom-call.0 | solution.py:160
  297.5 1.5 constant_dynamic-update-slice_fusion.5
  300.3 11.7 %cholesky.156 = f32[128,128]{1,0:T(8,128)S(1)} custom-call(f32[128,128]{1,0:T(8,128)S(1)} %copy.163), custom_call_target="Cholesky" | custom-call | tf_op jit(solution)/shard_map/jit(cholesky)/cholesky | solution.py:159
  314.0 9.8 %custom-call.14 = f32[1,128,128]{1,2,0:T(8,128)S(1)} custom-call(f32[1,128,128]{2,1,0:T(8,128)S(1)} %get-tuple-element.308), custom_call_target="InvertDiagBlocksLowerTriangular" | custom-call | tf_op jit(solution)/shard_map/triangular_solve/custom-call.0 | solution.py:160
  324.7 1.4 constant_dynamic-update-slice_fusion.4
  326.9 11.7 %cholesky.167 = f32[128,128]{1,0:T(8,128)S(1)} custom-call(f32[128,128]{1,0:T(8,128)S(1)} %fusion.105), custom_call_target="Cholesky" | custom-call | tf_op jit(solution)/shard_map/jit(cholesky)/cholesky | solution.py:159
  340.6 10.0 %custom-call.15 = f32[1,128,128]{1,2,0:T(8,128)S(1)} custom-call(f32[1,128,128]{2,1,0:T(8,128)S(1)} %get-tuple-element.306), custom_call_target="InvertDiagBlocksLowerTriangular" | custom-call | tf_op jit(solution)/shard_map/triangular_solve/custom-call.0 | solution.py:160
  353.3 5.5 fusion.31
  358.8 1.3 copy-done.2
  361.3 11.7 %cholesky.178 = f32[128,128]{1,0:T(8,128)S(1)} custom-call(f32[128,128]{1,0:T(8,128)S(1)} %fusion.103), custom_call_target="Cholesky" | custom-call | tf_op jit(solution)/shard_map/jit(cholesky)/cholesky | solution.py:159
  374.7 4.7 collective-permute-start
  380.6 9.8 %custom-call.16 = f32[1,128,128]{1,2,0:T(8,128)S(1)} custom-call(f32[1,128,128]{2,1,0:T(8,128)S(1)} %get-tuple-element.304), custom_call_target="InvertDiagBlocksLowerTriangular" | custom-call | tf_op jit(solution)/shard_map/triangular_solve/custom-call.0 | solution.py:160
  390.7 3.9 collective-permute-done
  395.3 1.9 constant_dynamic-update-slice_fusion.3
  397.3 1.7 fusion.37
  399.3 11.7 %cholesky.189 = f32[128,128]{1,0:T(8,128)S(1)} custom-call(f32[128,128]{1,0:T(8,128)S(1)} %fusion.101), custom_call_target="Cholesky" | custom-call | tf_op jit(solution)/shard_map/jit(cholesky)/cholesky | solution.py:159
  412.9 9.8 %custom-call.17 = f32[1,128,128]{1,2,0:T(8,128)S(1)} custom-call(f32[1,128,128]{2,1,0:T(8,128)S(1)} %get-tuple-element.302), custom_call_target="InvertDiagBlocksLowerTriangular" | custom-call | tf_op jit(solution)/shard_map/triangular_solve/custom-call.0 | solution.py:160
  424.7 12.1 %cholesky.200 = f32[128,128]{1,0:T(8,128)S(1)} custom-call(f32[128,128]{1,0:T(8,128)S(1)} %fusion.99), custom_call_target="Cholesky" | custom-call | tf_op jit(solution)/shard_map/jit(cholesky)/cholesky | solution.py:159
  438.6 9.8 %custom-call.18 = f32[1,128,128]{1,2,0:T(8,128)S(1)} custom-call(f32[1,128,128]{2,1,0:T(8,128)S(1)} %get-tuple-element.300), custom_call_target="InvertDiagBlocksLowerTriangular" | custom-call | tf_op jit(solution)/shard_map/triangular_solve/custom-call.0 | solution.py:160
  450.2 11.7 %cholesky.211 = f32[128,128]{1,0:T(8,128)S(1)} custom-call(f32[128,128]{1,0:T(8,128)S(1)} %fusion.97), custom_call_target="Cholesky" | custom-call | tf_op jit(solution)/shard_map/jit(cholesky)/cholesky | solution.py:159
  463.8 9.8 %custom-call.19 = f32[1,128,128]{1,2,0:T(8,128)S(1)} custom-call(f32[1,128,128]{2,1,0:T(8,128)S(1)} %get-tuple-element.298), custom_call_target="InvertDiagBlocksLowerTriangular" | custom-call | tf_op jit(solution)/shard_map/triangular_solve/custom-call.0 | solution.py:160
  479.6 3.1 fusion.42
  482.7 1.8 fusion.35
  484.6 1.5 fusion.163
  486.1 2.8 copy.143
  489.6 14.6 %fusion.2 = f32[3072,1024]{1,0:T(8,128)S(1)} fusion(bf16[2048,1024]{1,0:T(8,128)(2,1)S(1)} %bitcast.223, bf16[1024,1024]{1,0:T(8,128)(2,1)S(1)} %copy-done.9, f32[1,512,512]{2,1,0:T(8,128)S(1)} %copy-done.7, f32[1,512,512]{2,1,0:T(8,128)S(1)} %copy-done.6, f32[1,512,512]{2,1,0:T(8,128)S(1)} %fusion.35), kind=kOutput, calls=%fused_computation.9 | convolution fusion | flops 19344130048 | bytes 22020096 | tf_op jit(solution)/shard_map/dot_general | solution.py:206
  504.2 4.6 copy-done.4
  509.2 18.0 %fusion.15 = f32[1024,2048]{1,0:T(8,128)S(1)} fusion(f32[1024,2048]{1,0:T(8,128)} %bitcast_add_fusion, f32[3072,1024]{1,0:T(8,128)} %copy-done.4), kind=kOutput, calls=%fused_computation.27 | convolution fusion | flops 12886999040 | bytes 29360128 | tf_op jit(solution)/shard_map/dot_general | solution.py:42
  530.0 12.5 %copy.186 = f32[1,1024,1,2048]{3,2,1,0:T(1,128)} copy(f32[1,1024,1,2048]{3,1,2,0:T(8,128)S(1)} %select_bitcast_fusion) | data formatting | bytes 16777216 | tf_op jit(solution)/shard_map/broadcast_in_dim | solution.py:219
  (168 shorter events, 51.7 us)
Async XLA Ops:
  6.5 16.6 %copy-start = (bf16[64,128,128]{2,1,0:T(8,128)(2,1)S(1)}, bf16[64,128,128]{2,1,0:T(8,128)(2,1)}, u32[]{:S(2)}) copy-start(bf16[64,128,128]{2,1,0:T(8,128)(2,1)} %param.53) | copy-start | bytes 6291460
  11.4 33.0 %all-to-all-start = ((s32[128,1,2]{2,1,0:T(1,128)}), s32[128,1,2]{2,1,0:T(1,128)S(1)}, u32[]{:S(2)}, u32[]{:S(2)}) async-start(s32[128,1,2]{2,1,0:T(1,128)} %bitcast.4), calls=%async_computation | async-start | bytes 131072 | tf_op jit(solution)/shard_map/all_to_all | solution.py:83
  44.4 108.7 %all-to-all-start.1 = ((bf16[128,2,128,128]{3,2,1,0:T(8,128)(2,1)}), bf16[128,2,128,128]{3,2,1,0:T(8,128)(2,1)}, u32[]{:S(2)}, u32[]{:S(2)}) async-start(bf16[128,2,128,128]{3,2,1,0:T(8,128)(2,1)} %select_select_fusion), calls=%async_computation.1 | async-start | bytes 16777216 | tf_op jit(solution)/shard_map/all_to_all | solution.py:76
  54.6 186.1 %all-gather.6.cloned.1.call-start = ((), (), s32[]{:S(2)}) async-start(), calls=%async_computation.3 | async-start | bytes 2228224 | tf_op jit(solution)/shard_map/all_gather | solution.py:114
  162.1 39.7 %copy-start.5 = (bf16[1024,128]{1,0:T(8,128)(2,1)}, bf16[1024,128]{1,0:T(8,128)(2,1)S(1)}, u32[]{:S(2)}) copy-start(bf16[1024,128]{1,0:T(8,128)(2,1)S(1)} %slice_add_fusion) | copy-start | bytes 786436
  177.8 122.3 %all-gather.8.cloned.1.call-start = ((), (), s32[]{:S(2)}) async-start(), calls=%async_computation.4 | async-start | bytes 2228224 | tf_op jit(solution)/shard_map/all_gather | solution.py:116
  242.1 131.6 %all-gather.10.cloned.1.call-start = ((), (), s32[]{:S(2)}) async-start(), calls=%async_computation.5 | async-start | bytes 2359296 | tf_op jit(solution)/shard_map/all_gather | solution.py:119
  300.1 52.6 %slice-start = ((bf16[2048,512]{0,1:T(8,128)(2,1)}), bf16[1024,512]{0,1:T(8,128)(2,1)S(1)}, s32[]{:S(2)}) async-start(bf16[2048,512]{0,1:T(8,128)(2,1)} %all-gather.8.cloned.1.call-done), calls=%async_computation.7 | async-start | bytes 2097152 | tf_op jit(solution)/shard_map/slice | solution.py:116
  300.2 185.9 %all-gather.12.cloned.1.call-start = ((), (), s32[]{:S(2)}) async-start(), calls=%async_computation.6 | async-start | bytes 4456448 | tf_op jit(solution)/shard_map/all_gather | solution.py:131
  353.3 37.1 %copy-start.3 = (f32[8,128,128]{2,1,0:T(8,128)S(1)}, f32[8,128,128]{2,1,0:T(8,128)}, u32[]{:S(2)}) copy-start(f32[8,128,128]{2,1,0:T(8,128)} %get-tuple-element.327) | copy-start | bytes 1572868
  358.8 1.3 copy-start.2
  374.7 19.9 %collective-permute-start = (bf16[128,1024]{1,0:T(8,128)(2,1)S(1)}, bf16[128,1024]{1,0:T(8,128)(2,1)S(1)}, u32[]{:S(2)}, u32[]{:S(2)}) collective-permute-start(bf16[128,1024]{1,0:T(8,128)(2,1)S(1)} %constant_dynamic-slice_fusion), channel_id=1, source_target_pairs={{0,0},{1,8},{2,16},{3,24},{4,32},{5,40},{6,48},{7,56},{8,1},{9,9},... | collective-permute-start | bytes 786440 | tf_op jit(solution)/shard_map/ppermute | solution.py:130
  394.6 0.7 copy-start.8
  486.1 2.8 copy-start.6
  486.1 2.9 copy-start.7
  486.1 3.5 copy-start.9
  504.2 4.6 copy-start.4
  530.0 12.5 %copy-start.1 = (bf16[64,128,128]{2,1,0:T(8,128)(2,1)S(1)}, bf16[64,128,128]{2,1,0:T(8,128)(2,1)}, u32[]{:S(2)}) copy-start(bf16[64,128,128]{2,1,0:T(8,128)(2,1)} %param.53) | copy-start | bytes 6291460
Sparse Core Ops, SparseCore 0:
  177.9 46.6 all-gather.5
  242.2 47.1 all-gather.7
  300.3 28.9 all-gather.9
  395.5 51.5 all-gather.11
